TPU v7x, 32 devices: a whole 2x2x4 slice. The times are simulated.
32 devices in a mesh: gx: 2 (over core), ga: 4 (over y, x), gz: 4 (over z).
Axes of the slice: x: 2, y: 2, z: 4, core: 2. Of those that a mesh axis runs over, the one named last changes fastest.
Arguments:
- right_side: float32 [32, 64, 512], P('gx', 'ga', 'gz'), may hold values from -15 to 15
- diagonal: float32 [32, 64, 512], P('gx', 'ga', 'gz'), may hold values from 0.25 to 2
- basis_tables: float32 [3, 12, 12], replicated, may hold values from -1.75 to 1.75
- eigenvalues: float32 [3, 12], replicated, may hold values from 0.3 to 3
- coarse_blocks: float32 [2, 4, 4, 2, 64, 64], P('gx', 'ga', 'gz'), may hold values from -1 to 1
- coarse_columns: int32 [2, 4, 4, 2], P('gx', 'ga', 'gz'), may hold values from 0 to 15
Outputs:
- solution: float32 [32, 64, 512], P('gx', 'ga', 'gz')
- residual: float32 [32, 64, 512], P('gx', 'ga', 'gz')
All inputs are finite; a program needn't handle non-finite values.
Results may differ from a plain program's by a relative error of at most 0.0003.
Values sent between devices are 32-bit elements; how exact they have to be, the bound alone decides.
No kernel may reach another device: no remote copies, remote signals or barrier semaphores. Data moves between devices by JAX's collectives and lax.ppermute only.
A program may use at most 64 MiB of HBM per device.

v0:
```python
import jax
import jax.numpy as jnp
from jax import lax
from jax.sharding import PartitionSpec as P

PTS = 8
RIM = 2
WIDE = 12
CYCLES = 2


PRECISE = lax.Precision.HIGHEST


def padded_2(value, sides, width):
    for axis, dim in sides:
        size, length = (lax.axis_size(axis), value.shape[dim])
        up = [(i, (i + 1) % size) for i in range(size - 1)]
        down = [(j, i) for i, j in up]
        last = lax.slice_in_dim(value, length - width, length, axis=dim)
        leading = lax.slice_in_dim(value, 0, width, axis=dim)
        before = lax.ppermute(last, axis, up)
        after = lax.ppermute(leading, axis, down)
        value = jnp.concatenate([before, value, after], axis=dim)
    return value


def operate(field, diagonal):
    padded = padded_2(field, (("gx", 0), ("ga", 1), ("gz", 2)), 1)
    beside = padded[2:, 1:-1, 1:-1] + padded[:-2, 1:-1, 1:-1]
    beside = beside + padded[1:-1, 2:, 1:-1] + padded[1:-1, :-2, 1:-1]
    beside = beside + padded[1:-1, 1:-1, 2:] + padded[1:-1, 1:-1, :-2]
    return (6.0 + diagonal) * field - beside


def forward_table(count, basis):
    row_index = jnp.arange(PTS * count + 2 * RIM, dtype=jnp.int32)
    element = jnp.arange(count, dtype=jnp.int32)
    offset = jnp.arange(WIDE, dtype=jnp.int32)
    select = (
        row_index[:, None, None] == PTS * element[None, :, None] + offset[None, None, :]
    ).astype(jnp.float32)
    table = jnp.einsum("rcj,jm->rcm", select, basis, precision=PRECISE)
    return table.reshape(PTS * count + 2 * RIM, count * WIDE)


def backward_table(count, basis):
    same = jnp.eye(count, dtype=jnp.float32)
    table = jnp.einsum("cd,im->cmdi", same, basis[RIM : RIM + PTS], precision=PRECISE)
    return table.reshape(count * WIDE, count * PTS)


def schwarz_part(field, basis_tables, eigenvalues):
    count_x = field.shape[0] // PTS
    count_y = field.shape[1] // PTS
    count_z = field.shape[2] // PTS
    padded = padded_2(field, (("gx", 0), ("ga", 1), ("gz", 2)), RIM)
    spectral = jnp.einsum(
        "pqr,rc->pqc", padded, forward_table(count_z, basis_tables[2]), precision=PRECISE
    )
    spectral = jnp.einsum(
        "pqc,pa->aqc", spectral, forward_table(count_x, basis_tables[0]), precision=PRECISE
    )
    spectral = jnp.einsum(
        "aqc,qb->abc", spectral, forward_table(count_y, basis_tables[1]), precision=PRECISE
    )
    denominator = (
        jnp.tile(eigenvalues[0], count_x)[:, None, None]
        + jnp.tile(eigenvalues[1], count_y)[None, :, None]
    )
    denominator = denominator + jnp.tile(eigenvalues[2], count_z)[None, None, :]
    spectral = spectral / denominator
    local_part = jnp.einsum(
        "abc,cr->abr", spectral, backward_table(count_z, basis_tables[2]), precision=PRECISE
    )
    local_part = jnp.einsum(
        "abr,ap->pbr", local_part, backward_table(count_x, basis_tables[0]), precision=PRECISE
    )
    local_part = jnp.einsum(
        "pbr,bq->pqr", local_part, backward_table(count_y, basis_tables[1]), precision=PRECISE
    )
    return local_part


def coarse_part(field, blocks, selector):
    count_x = field.shape[0] // PTS
    count_y = field.shape[1] // PTS
    count_z = field.shape[2] // PTS
    cells = count_x * count_y * count_z
    means = jnp.mean(field.reshape(count_x, PTS, count_y, PTS, count_z, PTS), axis=(1, 3, 5))
    restricted = means.reshape(cells)
    terms = jnp.einsum("kpq,p->kq", blocks, restricted, precision=PRECISE)
    buffer = jnp.einsum("kj,kq->jq", selector, terms, precision=PRECISE)
    owned = lax.psum_scatter(buffer, ("ga", "gz"), scatter_dimension=0, tiled=True)
    whole = lax.all_gather(owned, ("ga", "gz"), axis=0, tiled=True)
    picked = jnp.dot(selector, whole, precision=PRECISE)
    coarse = jnp.einsum("kpq,kq->p", blocks, picked, precision=PRECISE)
    coarse = coarse.reshape(count_x, 1, count_y, 1, count_z, 1)
    spread = jnp.broadcast_to(coarse, (count_x, PTS, count_y, PTS, count_z, PTS))
    return spread.reshape(field.shape)


def start_norm(residual):
    return jnp.sqrt(lax.psum(jnp.sum(residual * residual), ("gx", "ga", "gz")))


def body(right_side, diagonal, basis_tables, eigenvalues, coarse_blocks, coarse_columns):
    blocks = coarse_blocks.reshape(coarse_blocks.shape[3:])
    columns = coarse_columns.reshape(coarse_columns.shape[3])
    group = lax.axis_size(("ga", "gz"))
    selector = (columns[:, None] == jnp.arange(group, dtype=jnp.int32)[None, :]).astype(jnp.float32)

    def precondition(field):
        return schwarz_part(field, basis_tables, eigenvalues) + coarse_part(field, blocks, selector)

    solution = jnp.zeros_like(right_side)
    residual = right_side
    for restart in range(CYCLES):
        initial_norm = start_norm(residual)
        first_vector = residual / initial_norm
        first_zed = precondition(first_vector)
        first_image = operate(first_zed, diagonal)
        first_proj, image_square = lax.psum(
            (jnp.sum(first_vector * first_image), jnp.sum(first_image * first_image)),
            ("gx", "ga", "gz"),
        )
        first_ortho = first_image - first_proj * first_vector
        first_len = jnp.sqrt(image_square - first_proj * first_proj)
        second_vector = first_ortho / first_len
        second_zed = precondition(second_vector)
        second_image = operate(second_zed, diagonal)
        upper_proj, lower_proj, second_square = lax.psum(
            (
                jnp.sum(first_vector * second_image),
                jnp.sum(second_vector * second_image),
                jnp.sum(second_image * second_image),
            ),
            ("gx", "ga", "gz"),
        )
        second_len = jnp.sqrt(second_square - upper_proj * upper_proj - lower_proj * lower_proj)
        gram_first = first_proj * first_proj + first_len * first_len
        gram_cross = first_proj * upper_proj + first_len * lower_proj
        gram_second = upper_proj * upper_proj + lower_proj * lower_proj + second_len * second_len
        target_first = initial_norm * first_proj
        target_second = initial_norm * upper_proj
        determinant = gram_first * gram_second - gram_cross * gram_cross
        weight_first = (gram_second * target_first - gram_cross * target_second) / determinant
        weight_second = (gram_first * target_second - gram_cross * target_first) / determinant
        solution = solution + weight_first * first_zed + weight_second * second_zed
        residual = right_side - operate(solution, diagonal)
    return (solution, residual)


def solution(mesh):
    in_specs = (
        P("gx", "ga", "gz"),
        P("gx", "ga", "gz"),
        P(),
        P(),
        P("gx", "ga", "gz", None, None, None),
        P("gx", "ga", "gz", None),
    )
    out_specs = (P("gx", "ga", "gz"), P("gx", "ga", "gz"))
    return jax.shard_map(body, mesh=mesh, in_specs=in_specs, out_specs=out_specs, check_vma=False)
```

profile of v0, /device:TPU:0, one launch (start us, length us, event | category | flops | bytes accessed | tf_op | source)
XLA Modules:
  0.0 854.5 jit_solution(14189468546565872897)
XLA Ops:
  2.2 42.2 %psum.84 = f32[]{:T(128)} all-reduce(f32[]{:T(128)} %multiply_reduce_fusion.11), channel_id=1, replica_groups=mesh['gx'=2,'ga'=4,'gz'=4] {'gx','ga','gz'}, use_global_device_ids=true, to_apply=%region_1.0 | all-reduce | flops 1 | bytes 8 | tf_op jit(solution)/shard_map/psum | solution.py:104
  51.4 41.6 %all-reduce = f32[16,64]{1,0:T(8,128)S(1)} all-reduce(f32[16,64]{1,0:T(8,128)S(1)} %fusion.102), channel_id=2, replica_groups=mesh['gx'=2,'ga'=4,'gz'=4] {'ga','gz'}, use_global_device_ids=true, to_apply=%region_3.0.clone | all-reduce | flops 1024 | bytes 8192
  94.3 35.3 %all-gather = f32[16,1,64]{2,1,0:T(1,128)S(1)} all-gather(f32[1,1,64]{2,1,0:T(1,128)S(1)} %fusion.103), channel_id=1, replica_groups=mesh['gx'=2,'ga'=4,'gz'=4] {'ga','gz'}, dimensions={0}, use_global_device_ids=true | all-gather | bytes 4352 | tf_op jit(solution)/shard_map/all_gather | solution.py:95
  133.4 5.4 collective-permute-done.3
  162.1 5.4 collective-permute-start.9
  170.3 4.6 collective-permute-start.11
  179.8 42.5 %all-reduce.7 = (f32[]{:T(128)}, f32[]{:T(128)}) all-reduce(f32[]{:T(128)} %get-tuple-element.11, f32[]{:T(128)} %get-tuple-element.10), channel_id=1, replica_groups=mesh['gx'=2,'ga'=4,'gz'=4] {'gx','ga','gz'}, use_global_device_ids=true, to_apply=%region_7.0 | all-reduce | flops 2 | bytes 16 | tf_op jit(solution)/shard_map/psum | solution.py:123
  229.3 42.4 %all-reduce.1 = f32[16,64]{1,0:T(8,128)S(1)} all-reduce(f32[16,64]{1,0:T(8,128)S(1)} %fusion.100), channel_id=3, replica_groups=mesh['gx'=2,'ga'=4,'gz'=4] {'ga','gz'}, use_global_device_ids=true, to_apply=%region_9.0.clone | all-reduce | flops 1024 | bytes 8192
  272.4 35.3 %all-gather.1 = f32[16,1,64]{2,1,0:T(1,128)S(1)} all-gather(f32[1,1,64]{2,1,0:T(1,128)S(1)} %fusion.104), channel_id=1, replica_groups=mesh['gx'=2,'ga'=4,'gz'=4] {'ga','gz'}, dimensions={0}, use_global_device_ids=true | all-gather | bytes 4352 | tf_op jit(solution)/shard_map/all_gather | solution.py:95
  339.2 5.4 collective-permute-start.21
  357.0 42.6 %all-reduce.6 = (f32[]{:T(128)}, f32[]{:T(128)}, f32[]{:T(128)}) all-reduce(f32[]{:T(128)} %get-tuple-element.9, f32[]{:T(128)} %get-tuple-element.8, f32[]{:T(128)} %get-tuple-element.7), channel_id=1, replica_groups=mesh['gx'=2,'ga'=4,'gz'=4] {'gx','ga','gz'}, use_global_device_ids=true, to_apply=%region_11.0 | all-reduce | flops 3 | bytes 24 | tf_op jit(solution)/shard_map/psum | solution.py:132
  411.9 4.8 collective-permute-start.27
  429.0 42.5 %psum.90 = f32[]{:T(128)} all-reduce(f32[]{:T(128)} %get-tuple-element.23), channel_id=1, replica_groups=mesh['gx'=2,'ga'=4,'gz'=4] {'gx','ga','gz'}, use_global_device_ids=true, to_apply=%region_17.0 | all-reduce | flops 1 | bytes 8 | tf_op jit(solution)/shard_map/psum | solution.py:104
  476.7 42.4 %all-reduce.2 = f32[16,64]{1,0:T(8,128)S(1)} all-reduce(f32[16,64]{1,0:T(8,128)S(1)} %fusion.98), channel_id=4, replica_groups=mesh['gx'=2,'ga'=4,'gz'=4] {'ga','gz'}, use_global_device_ids=true, to_apply=%region_19.0.clone | all-reduce | flops 1024 | bytes 8192
  519.7 35.3 %all-gather.2 = f32[16,1,64]{2,1,0:T(1,128)S(1)} all-gather(f32[1,1,64]{2,1,0:T(1,128)S(1)} %fusion.105), channel_id=1, replica_groups=mesh['gx'=2,'ga'=4,'gz'=4] {'ga','gz'}, dimensions={0}, use_global_device_ids=true | all-gather | bytes 4352 | tf_op jit(solution)/shard_map/all_gather | solution.py:95
  586.5 5.5 collective-permute-start.39
  604.2 42.5 %all-reduce.5 = (f32[]{:T(128)}, f32[]{:T(128)}) all-reduce(f32[]{:T(128)} %get-tuple-element.6, f32[]{:T(128)} %get-tuple-element.5), channel_id=1, replica_groups=mesh['gx'=2,'ga'=4,'gz'=4] {'gx','ga','gz'}, use_global_device_ids=true, to_apply=%region_23.0 | all-reduce | flops 2 | bytes 16 | tf_op jit(solution)/shard_map/psum | solution.py:123
  653.9 42.4 %all-reduce.3 = f32[16,64]{1,0:T(8,128)S(1)} all-reduce(f32[16,64]{1,0:T(8,128)S(1)} %fusion.96), channel_id=5, replica_groups=mesh['gx'=2,'ga'=4,'gz'=4] {'ga','gz'}, use_global_device_ids=true, to_apply=%region_25.0.clone | all-reduce | flops 1024 | bytes 8192
  697.0 35.3 %all-gather.3 = f32[16,1,64]{2,1,0:T(1,128)S(1)} all-gather(f32[1,1,64]{2,1,0:T(1,128)S(1)} %fusion.106), channel_id=1, replica_groups=mesh['gx'=2,'ga'=4,'gz'=4] {'ga','gz'}, dimensions={0}, use_global_device_ids=true | all-gather | bytes 4352 | tf_op jit(solution)/shard_map/all_gather | solution.py:95
  740.4 4.6 collective-permute-start.46
  748.3 5.1 collective-permute-done.47
  764.5 5.5 collective-permute-start.51
  782.3 42.6 %all-reduce.4 = (f32[]{:T(128)}, f32[]{:T(128)}, f32[]{:T(128)}) all-reduce(f32[]{:T(128)} %get-tuple-element.4, f32[]{:T(128)} %get-tuple-element.3, f32[]{:T(128)} %get-tuple-element.2), channel_id=1, replica_groups=mesh['gx'=2,'ga'=4,'gz'=4] {'gx','ga','gz'}, use_global_device_ids=true, to_apply=%region_27.0 | all-reduce | flops 3 | bytes 24 | tf_op jit(solution)/shard_map/psum | solution.py:132
  837.0 4.8 collective-permute-start.57
  (314 shorter events, 217.9 us)
Async XLA Ops:
  46.1 84.5 %collective-permute-start = (f32[2,16,128]{2,1,0:T(8,128)S(1)}, f32[2,16,128]{2,1,0:T(8,128)S(1)}, u32[]{:S(2)}, u32[]{:S(2)}) collective-permute-start(f32[2,16,128]{2,1,0:T(8,128)S(1)} %get-tuple-element.84), channel_id=1, source_target_pairs={{0,16},{1,17},{2,18},{3,19},{4,20},{5,21},{6,22},{7,23},{8,24},{9,... | collective-permute-start | bytes 49160 | tf_op jit(solution)/shard_map/ppermute | solution.py:22
  47.3 83.2 %collective-permute-start.1 = (f32[2,16,128]{2,1,0:T(8,128)S(1)}, f32[2,16,128]{2,1,0:T(8,128)S(1)}, u32[]{:S(2)}, u32[]{:S(2)}) collective-permute-start(f32[2,16,128]{2,1,0:T(8,128)S(1)} %get-tuple-element.85), channel_id=1, source_target_pairs={{16,0},{17,1},{18,2},{19,3},{20,4},{21,5},{22,6},{23,7},{24,8},{25... | collective-permute-start | bytes 49160 | tf_op jit(solution)/shard_map/ppermute | solution.py:23
  143.7 8.3 collective-permute-start.5
  169.0 8.7 %collective-permute-start.10 = (f32[18,18,1]{2,1,0:T(8,128)S(1)}, f32[18,18,1]{2,1,0:T(8,128)S(1)}, u32[]{:S(2)}, u32[]{:S(2)}) collective-permute-start(f32[18,18,1]{2,1,0:T(8,128)S(1)} %get-tuple-element.44), channel_id=1, source_target_pairs={{1,0},{2,1},{3,2},{5,4},{6,5},{7,6},{9,8},{10,9},{11,10},{13,12},{... | collective-permute-start | bytes 3896 | tf_op jit(solution)/shard_map/ppermute | solution.py:23
  170.3 8.6 %collective-permute-start.11 = (f32[18,18,1]{2,1,0:T(8,128)S(1)}, f32[18,18,1]{2,1,0:T(8,128)S(1)}, u32[]{:S(2)}, u32[]{:S(2)}) collective-permute-start(f32[18,18,1]{2,1,0:T(8,128)S(1)} %get-tuple-element.45), channel_id=1, source_target_pairs={{0,1},{1,2},{2,3},{4,5},{5,6},{6,7},{8,9},{9,10},{10,11},{12,13},{... | collective-permute-start | bytes 3896 | tf_op jit(solution)/shard_map/ppermute | solution.py:22
  226.0 81.7 %collective-permute-start.12 = (f32[2,16,128]{2,1,0:T(8,128)S(1)}, f32[2,16,128]{2,1,0:T(8,128)S(1)}, u32[]{:S(2)}, u32[]{:S(2)}) collective-permute-start(f32[2,16,128]{2,1,0:T(8,128)S(1)} %get-tuple-element.80), channel_id=1, source_target_pairs={{0,16},{1,17},{2,18},{3,19},{4,20},{5,21},{6,22},{7,23},{8,24},{9,... | collective-permute-start | bytes 49160 | tf_op jit(solution)/shard_map/ppermute | solution.py:22
  227.3 80.4 %collective-permute-start.13 = (f32[2,16,128]{2,1,0:T(8,128)S(1)}, f32[2,16,128]{2,1,0:T(8,128)S(1)}, u32[]{:S(2)}, u32[]{:S(2)}) collective-permute-start(f32[2,16,128]{2,1,0:T(8,128)S(1)} %get-tuple-element.81), channel_id=1, source_target_pairs={{16,0},{17,1},{18,2},{19,3},{20,4},{21,5},{22,6},{23,7},{24,8},{25... | collective-permute-start | bytes 49160 | tf_op jit(solution)/shard_map/ppermute | solution.py:23
  319.8 8.4 collective-permute-start.17
  346.2 8.7 %collective-permute-start.22 = (f32[18,18,1]{2,1,0:T(8,128)S(1)}, f32[18,18,1]{2,1,0:T(8,128)S(1)}, u32[]{:S(2)}, u32[]{:S(2)}) collective-permute-start(f32[18,18,1]{2,1,0:T(8,128)S(1)} %get-tuple-element.42), channel_id=1, source_target_pairs={{1,0},{2,1},{3,2},{5,4},{6,5},{7,6},{9,8},{10,9},{11,10},{13,12},{... | collective-permute-start | bytes 3896 | tf_op jit(solution)/shard_map/ppermute | solution.py:23
  347.5 8.6 %collective-permute-start.23 = (f32[18,18,1]{2,1,0:T(8,128)S(1)}, f32[18,18,1]{2,1,0:T(8,128)S(1)}, u32[]{:S(2)}, u32[]{:S(2)}) collective-permute-start(f32[18,18,1]{2,1,0:T(8,128)S(1)} %get-tuple-element.43), channel_id=1, source_target_pairs={{0,1},{1,2},{2,3},{4,5},{5,6},{6,7},{8,9},{9,10},{10,11},{12,13},{... | collective-permute-start | bytes 3896 | tf_op jit(solution)/shard_map/ppermute | solution.py:22
  418.2 8.7 %collective-permute-start.28 = (f32[18,18,1]{2,1,0:T(8,128)S(1)}, f32[18,18,1]{2,1,0:T(8,128)S(1)}, u32[]{:S(2)}, u32[]{:S(2)}) collective-permute-start(f32[18,18,1]{2,1,0:T(8,128)S(1)} %get-tuple-element.40), channel_id=1, source_target_pairs={{1,0},{2,1},{3,2},{5,4},{6,5},{7,6},{9,8},{10,9},{11,10},{13,12},{... | collective-permute-start | bytes 3896 | tf_op jit(solution)/shard_map/ppermute | solution.py:23
  419.5 8.6 %collective-permute-start.29 = (f32[18,18,1]{2,1,0:T(8,128)S(1)}, f32[18,18,1]{2,1,0:T(8,128)S(1)}, u32[]{:S(2)}, u32[]{:S(2)}) collective-permute-start(f32[18,18,1]{2,1,0:T(8,128)S(1)} %get-tuple-element.41), channel_id=1, source_target_pairs={{0,1},{1,2},{2,3},{4,5},{5,6},{6,7},{8,9},{9,10},{10,11},{12,13},{... | collective-permute-start | bytes 3896 | tf_op jit(solution)/shard_map/ppermute | solution.py:22
  473.3 81.7 %collective-permute-start.30 = (f32[2,16,128]{2,1,0:T(8,128)S(1)}, f32[2,16,128]{2,1,0:T(8,128)S(1)}, u32[]{:S(2)}, u32[]{:S(2)}) collective-permute-start(f32[2,16,128]{2,1,0:T(8,128)S(1)} %get-tuple-element.74), channel_id=1, source_target_pairs={{0,16},{1,17},{2,18},{3,19},{4,20},{5,21},{6,22},{7,23},{8,24},{9,... | collective-permute-start | bytes 49160 | tf_op jit(solution)/shard_map/ppermute | solution.py:22
  474.6 80.4 %collective-permute-start.31 = (f32[2,16,128]{2,1,0:T(8,128)S(1)}, f32[2,16,128]{2,1,0:T(8,128)S(1)}, u32[]{:S(2)}, u32[]{:S(2)}) collective-permute-start(f32[2,16,128]{2,1,0:T(8,128)S(1)} %get-tuple-element.75), channel_id=1, source_target_pairs={{16,0},{17,1},{18,2},{19,3},{20,4},{21,5},{22,6},{23,7},{24,8},{25... | collective-permute-start | bytes 49160 | tf_op jit(solution)/shard_map/ppermute | solution.py:23
  567.1 8.4 collective-permute-start.35
  593.5 8.7 %collective-permute-start.40 = (f32[18,18,1]{2,1,0:T(8,128)S(1)}, f32[18,18,1]{2,1,0:T(8,128)S(1)}, u32[]{:S(2)}, u32[]{:S(2)}) collective-permute-start(f32[18,18,1]{2,1,0:T(8,128)S(1)} %get-tuple-element.38), channel_id=1, source_target_pairs={{1,0},{2,1},{3,2},{5,4},{6,5},{7,6},{9,8},{10,9},{11,10},{13,12},{... | collective-permute-start | bytes 3896 | tf_op jit(solution)/shard_map/ppermute | solution.py:23
  594.8 8.6 %collective-permute-start.41 = (f32[18,18,1]{2,1,0:T(8,128)S(1)}, f32[18,18,1]{2,1,0:T(8,128)S(1)}, u32[]{:S(2)}, u32[]{:S(2)}) collective-permute-start(f32[18,18,1]{2,1,0:T(8,128)S(1)} %get-tuple-element.39), channel_id=1, source_target_pairs={{0,1},{1,2},{2,3},{4,5},{5,6},{6,7},{8,9},{9,10},{10,11},{12,13},{... | collective-permute-start | bytes 3896 | tf_op jit(solution)/shard_map/ppermute | solution.py:22
  650.6 81.7 %collective-permute-start.42 = (f32[2,16,128]{2,1,0:T(8,128)S(1)}, f32[2,16,128]{2,1,0:T(8,128)S(1)}, u32[]{:S(2)}, u32[]{:S(2)}) collective-permute-start(f32[2,16,128]{2,1,0:T(8,128)S(1)} %get-tuple-element.70), channel_id=1, source_target_pairs={{0,16},{1,17},{2,18},{3,19},{4,20},{5,21},{6,22},{7,23},{8,24},{9,... | collective-permute-start | bytes 49160 | tf_op jit(solution)/shard_map/ppermute | solution.py:22
  651.9 80.4 %collective-permute-start.43 = (f32[2,16,128]{2,1,0:T(8,128)S(1)}, f32[2,16,128]{2,1,0:T(8,128)S(1)}, u32[]{:S(2)}, u32[]{:S(2)}) collective-permute-start(f32[2,16,128]{2,1,0:T(8,128)S(1)} %get-tuple-element.71), channel_id=1, source_target_pairs={{16,0},{17,1},{18,2},{19,3},{20,4},{21,5},{22,6},{23,7},{24,8},{25... | collective-permute-start | bytes 49160 | tf_op jit(solution)/shard_map/ppermute | solution.py:23
  745.0 8.4 collective-permute-start.47
  771.5 8.7 %collective-permute-start.52 = (f32[18,18,1]{2,1,0:T(8,128)S(1)}, f32[18,18,1]{2,1,0:T(8,128)S(1)}, u32[]{:S(2)}, u32[]{:S(2)}) collective-permute-start(f32[18,18,1]{2,1,0:T(8,128)S(1)} %get-tuple-element.36), channel_id=1, source_target_pairs={{1,0},{2,1},{3,2},{5,4},{6,5},{7,6},{9,8},{10,9},{11,10},{13,12},{... | collective-permute-start | bytes 3896 | tf_op jit(solution)/shard_map/ppermute | solution.py:23
  772.8 8.6 %collective-permute-start.53 = (f32[18,18,1]{2,1,0:T(8,128)S(1)}, f32[18,18,1]{2,1,0:T(8,128)S(1)}, u32[]{:S(2)}, u32[]{:S(2)}) collective-permute-start(f32[18,18,1]{2,1,0:T(8,128)S(1)} %get-tuple-element.37), channel_id=1, source_target_pairs={{0,1},{1,2},{2,3},{4,5},{5,6},{6,7},{8,9},{9,10},{10,11},{12,13},{... | collective-permute-start | bytes 3896 | tf_op jit(solution)/shard_map/ppermute | solution.py:22
  843.3 8.7 %collective-permute-start.58 = (f32[18,18,1]{2,1,0:T(8,128)S(1)}, f32[18,18,1]{2,1,0:T(8,128)S(1)}, u32[]{:S(2)}, u32[]{:S(2)}) collective-permute-start(f32[18,18,1]{2,1,0:T(8,128)S(1)} %get-tuple-element.34), channel_id=1, source_target_pairs={{1,0},{2,1},{3,2},{5,4},{6,5},{7,6},{9,8},{10,9},{11,10},{13,12},{... | collective-permute-start | bytes 3896 | tf_op jit(solution)/shard_map/ppermute | solution.py:23
  844.6 8.6 %collective-permute-start.59 = (f32[18,18,1]{2,1,0:T(8,128)S(1)}, f32[18,18,1]{2,1,0:T(8,128)S(1)}, u32[]{:S(2)}, u32[]{:S(2)}) collective-permute-start(f32[18,18,1]{2,1,0:T(8,128)S(1)} %get-tuple-element.35), channel_id=1, source_target_pairs={{0,1},{1,2},{2,3},{4,5},{5,6},{6,7},{8,9},{9,10},{10,11},{12,13},{... | collective-permute-start | bytes 3896 | tf_op jit(solution)/shard_map/ppermute | solution.py:22
  (62 other events, 656.1 us)
where the time goes:
time: 868 us; the launch traced here: 855 us
  blocking collectives  565 us (65%)
  starting transfers between devices  143 us (16%)
  waiting for transfers between devices  74.9 us (9%)
  between operations  20.7 us (2%)
  local copies, waits for them, and re-layouts  18.6 us (2%)
  matrix products  17.2 us (2%)
  other arithmetic  15.3 us (2%)
    unnamed x4, blocking collectives  169 us
    all_gather x4, blocking collectives, coarse_part(): whole = lax.all_gather(owned, ('ga', 'gz'), axis=0, tiled=True)  141 us
    ppermute x30, starting transfers between devices, padded_2(): before = lax.ppermute(last, axis, up)  104 us
    psum x2, blocking collectives, body(): lax.psum((jnp.sum(first_vector * second_image), jnp.sum(second_vector * s...  85.1 us
    psum x2, blocking collectives, body(): lax.psum((jnp.sum(first_vector * first_image), jnp.sum(first_image * firs...  85.1 us
    psum x2, blocking collectives, start_norm(): return jnp.sqrt(lax.psum(jnp.sum(residual * residual), ('gx', 'ga', 'gz')))  84.7 us
    ppermute x30, waiting for transfers between devices, padded_2(): after = lax.ppermute(leading, axis, down)  52.6 us
    ppermute x30, starting transfers between devices, padded_2(): after = lax.ppermute(leading, axis, down)  39.4 us
  transfers between devices with their start and end apart: 60, of which 36 were waited for; matrix products, arithmetic and copies ran while one was open for 2% of the time, Pallas kernels for 0%

commit v1 on v0

--- a/solution.py
+++ b/solution.py
@@ -82,7 +82,7 @@
     return local_part
 
 
-def coarse_part(field, blocks, selector):
+def coarse_terms(field, blocks, selector):
     count_x = field.shape[0] // PTS
     count_y = field.shape[1] // PTS
     count_z = field.shape[2] // PTS
@@ -90,18 +90,35 @@
     means = jnp.mean(field.reshape(count_x, PTS, count_y, PTS, count_z, PTS), axis=(1, 3, 5))
     restricted = means.reshape(cells)
     terms = jnp.einsum("kpq,p->kq", blocks, restricted, precision=PRECISE)
-    buffer = jnp.einsum("kj,kq->jq", selector, terms, precision=PRECISE)
-    owned = lax.psum_scatter(buffer, ("ga", "gz"), scatter_dimension=0, tiled=True)
-    whole = lax.all_gather(owned, ("ga", "gz"), axis=0, tiled=True)
+    return jnp.einsum("kj,kq->jq", selector, terms, precision=PRECISE)
+
+
+def coarse_apply(whole, blocks, selector, shape):
+    count_x = shape[0] // PTS
+    count_y = shape[1] // PTS
+    count_z = shape[2] // PTS
     picked = jnp.dot(selector, whole, precision=PRECISE)
     coarse = jnp.einsum("kpq,kq->p", blocks, picked, precision=PRECISE)
     coarse = coarse.reshape(count_x, 1, count_y, 1, count_z, 1)
     spread = jnp.broadcast_to(coarse, (count_x, PTS, count_y, PTS, count_z, PTS))
-    return spread.reshape(field.shape)
+    return spread.reshape(shape)
 
 
-def start_norm(residual):
-    return jnp.sqrt(lax.psum(jnp.sum(residual * residual), ("gx", "ga", "gz")))
+ALL = ("gx", "ga", "gz")
+
+
+def reduce_all(buffer, scalars):
+    n_gx = lax.axis_size("gx")
+    me = lax.axis_index("gx")
+    slot = (jnp.arange(n_gx, dtype=jnp.int32) == me).astype(jnp.float32)
+    parts = [] if buffer is None else [(slot[:, None, None] * buffer[None]).reshape(-1)]
+    payload = jnp.concatenate(parts + [jnp.stack(scalars)])
+    total = lax.psum(payload, ALL)
+    sums = [total[total.shape[0] - len(scalars) + i] for i in range(len(scalars))]
+    if buffer is None:
+        return None, sums
+    wide = total[: total.shape[0] - len(scalars)].reshape((n_gx,) + buffer.shape)
+    return lax.dynamic_index_in_dim(wide, me, 0, keepdims=False), sums
 
 
 def body(right_side, diagonal, basis_tables, eigenvalues, coarse_blocks, coarse_columns):
@@ -109,33 +126,39 @@
     columns = coarse_columns.reshape(coarse_columns.shape[3])
     group = lax.axis_size(("ga", "gz"))
     selector = (columns[:, None] == jnp.arange(group, dtype=jnp.int32)[None, :]).astype(jnp.float32)
-
-    def precondition(field):
-        return schwarz_part(field, basis_tables, eigenvalues) + coarse_part(field, blocks, selector)
+    shape = right_side.shape
 
     solution = jnp.zeros_like(right_side)
     residual = right_side
     for restart in range(CYCLES):
-        initial_norm = start_norm(residual)
+        whole_r, (square,) = reduce_all(
+            coarse_terms(residual, blocks, selector), [jnp.sum(residual * residual)]
+        )
+        initial_norm = jnp.sqrt(square)
         first_vector = residual / initial_norm
-        first_zed = precondition(first_vector)
+        first_zed = (
+            schwarz_part(residual, basis_tables, eigenvalues)
+            + coarse_apply(whole_r, blocks, selector, shape)
+        ) / initial_norm
         first_image = operate(first_zed, diagonal)
-        first_proj, image_square = lax.psum(
-            (jnp.sum(first_vector * first_image), jnp.sum(first_image * first_image)),
-            ("gx", "ga", "gz"),
+        whole_w, (first_proj, image_square) = reduce_all(
+            coarse_terms(first_image, blocks, selector),
+            [jnp.sum(first_vector * first_image), jnp.sum(first_image * first_image)],
         )
-        first_ortho = first_image - first_proj * first_vector
         first_len = jnp.sqrt(image_square - first_proj * first_proj)
-        second_vector = first_ortho / first_len
-        second_zed = precondition(second_vector)
+        image_zed = schwarz_part(first_image, basis_tables, eigenvalues) + coarse_apply(
+            whole_w, blocks, selector, shape
+        )
+        second_vector = (first_image - first_proj * first_vector) / first_len
+        second_zed = (image_zed - first_proj * first_zed) / first_len
         second_image = operate(second_zed, diagonal)
-        upper_proj, lower_proj, second_square = lax.psum(
-            (
+        _, (upper_proj, lower_proj, second_square) = reduce_all(
+            None,
+            [
                 jnp.sum(first_vector * second_image),
                 jnp.sum(second_vector * second_image),
                 jnp.sum(second_image * second_image),
-            ),
-            ("gx", "ga", "gz"),
+            ],
         )
         second_len = jnp.sqrt(second_square - upper_proj * upper_proj - lower_proj * lower_proj)
         gram_first = first_proj * first_proj + first_len * first_len

time: 868 us -> 562 us (0.65)
  the two profiles are of different devices: /device:TPU:0 before, /device:TPU:10 now
where the time goes in v1:
time: 562 us; the launch traced here: 551 us
  blocking collectives  241 us (43%)
  starting transfers between devices  146 us (26%)
  waiting for transfers between devices  77.8 us (14%)
  local copies, waits for them, and re-layouts  24.6 us (4%)
  matrix products  24.5 us (4%)
  between operations  20.9 us (4%)
  other arithmetic  15.6 us (3%)
    psum x6, blocking collectives, reduce_all(): total = lax.psum(payload, ALL)  241 us
    ppermute x30, starting transfers between devices, padded_2(): before = lax.ppermute(last, axis, up)  75.1 us
    ppermute x30, starting transfers between devices, padded_2(): after = lax.ppermute(leading, axis, down)  71.2 us
    ppermute x30, waiting for transfers between devices, padded_2(): after = lax.ppermute(leading, axis, down)  61.5 us
    ppermute x30, waiting for transfers between devices, padded_2(): before = lax.ppermute(last, axis, up)  16.3 us
  transfers between devices with their start and end apart: 60, of which 32 were waited for; matrix products, arithmetic and copies ran while one was open for 5% of the time, Pallas kernels for 0%

profile of v1, /device:TPU:10, one launch (start us, length us, event | category | flops | bytes accessed | tf_op | source)
XLA Modules:
  0.0 551.1 jit_solution(13104727968925354297)
XLA Ops:
  14.7 3.4 collective-permute-start.2
  21.2 41.4 %psum.42 = f32[2049]{0:T(1024)S(1)} all-reduce(f32[2049]{0:T(1024)S(1)} %pad_maximum_fusion.127), channel_id=1, replica_groups=mesh['gx'=2,'ga'=4,'gz'=4] {'gx','ga','gz'}, use_global_device_ids=true, to_apply=%region_2.0 | all-reduce | flops 2049 | bytes 16392 | tf_op jit(solution)/shard_map/psum | solution.py:116
  83.9 3.4 collective-permute-start.9
  89.7 4.0 collective-permute-done.8
  111.1 39.6 %psum.43 = f32[2050]{0:T(1024)S(1)} all-reduce(f32[2050]{0:T(1024)S(1)} %concatenate.213), channel_id=1, replica_groups=mesh['gx'=2,'ga'=4,'gz'=4] {'gx','ga','gz'}, use_global_device_ids=true, to_apply=%region_6.7 | all-reduce | flops 2050 | bytes 16400 | tf_op jit(solution)/shard_map/psum | solution.py:116
  151.0 3.4 collective-permute-start.14
  157.2 3.8 collective-permute-done.15
  185.1 3.9 collective-permute-start.20
  205.8 40.5 %psum.44 = f32[3]{0:T(128)S(1)} all-reduce(f32[3]{0:T(128)S(1)} %pad_maximum_fusion.147), channel_id=1, replica_groups=mesh['gx'=2,'ga'=4,'gz'=4] {'gx','ga','gz'}, use_global_device_ids=true, to_apply=%region_10.11 | all-reduce | flops 3 | bytes 24 | tf_op jit(solution)/shard_map/psum | solution.py:116
  257.4 3.4 collective-permute-start.27
  263.3 4.0 collective-permute-done.26
  269.7 3.5 collective-permute-start.29
  283.6 40.9 %psum.45 = f32[2049]{0:T(1024)S(1)} all-reduce(f32[2049]{0:T(1024)S(1)} %pad_maximum_fusion.128), channel_id=1, replica_groups=mesh['gx'=2,'ga'=4,'gz'=4] {'gx','ga','gz'}, use_global_device_ids=true, to_apply=%region_13.14 | all-reduce | flops 2049 | bytes 16392 | tf_op jit(solution)/shard_map/psum | solution.py:116
  324.7 3.4 collective-permute-start.32
  330.7 3.9 collective-permute-done.33
  338.8 3.4 collective-permute-start.35
  358.3 3.9 collective-permute-start.38
  383.0 39.2 %psum.46 = f32[2050]{0:T(1024)S(1)} all-reduce(f32[2050]{0:T(1024)S(1)} %concatenate.245), channel_id=1, replica_groups=mesh['gx'=2,'ga'=4,'gz'=4] {'gx','ga','gz'}, use_global_device_ids=true, to_apply=%region_17.18 | all-reduce | flops 2050 | bytes 16400 | tf_op jit(solution)/shard_map/psum | solution.py:116
  422.4 3.4 collective-permute-start.44
  428.6 3.8 collective-permute-done.45
  436.6 3.5 collective-permute-start.47
  456.7 3.9 collective-permute-start.50
  478.0 39.6 %psum.47 = f32[3]{0:T(128)S(1)} all-reduce(f32[3]{0:T(128)S(1)} %pad_maximum_fusion.148), channel_id=1, replica_groups=mesh['gx'=2,'ga'=4,'gz'=4] {'gx','ga','gz'}, use_global_device_ids=true, to_apply=%region_21.22 | all-reduce | flops 3 | bytes 24 | tf_op jit(solution)/shard_map/psum | solution.py:116
  534.6 4.0 collective-permute-done.56
  (288 shorter events, 223.0 us)
Async XLA Ops:
  1.4 13.2 %collective-permute-start.1 = (f32[2,16,128]{2,1,0:T(8,128)S(1)}, f32[2,16,128]{2,1,0:T(8,128)S(1)}, u32[]{:S(2)}, u32[]{:S(2)}) collective-permute-start(f32[2,16,128]{2,1,0:T(8,128)S(1)} %get-tuple-element.74), channel_id=1, source_target_pairs={{16,0},{17,1},{18,2},{19,3},{20,4},{21,5},{22,6},{23,7},{24,8},{25... | collective-permute-start | bytes 49160 | tf_op jit(solution)/shard_map/ppermute | solution.py:23
  2.7 11.3 %collective-permute-start = (f32[2,16,128]{2,1,0:T(8,128)S(1)}, f32[2,16,128]{2,1,0:T(8,128)S(1)}, u32[]{:S(2)}, u32[]{:S(2)}) collective-permute-start(f32[2,16,128]{2,1,0:T(8,128)S(1)} %get-tuple-element.75), channel_id=1, source_target_pairs={{0,16},{1,17},{2,18},{3,19},{4,20},{5,21},{6,22},{7,23},{8,24},{9,... | collective-permute-start | bytes 49160 | tf_op jit(solution)/shard_map/ppermute | solution.py:22
  14.7 48.2 %collective-permute-start.2 = (f32[20,2,128]{2,1,0:T(2,128)S(1)}, f32[20,2,128]{2,1,0:T(2,128)S(1)}, u32[]{:S(2)}, u32[]{:S(2)}) collective-permute-start(f32[20,2,128]{2,1,0:T(2,128)S(1)} %get-tuple-element.42), channel_id=1, source_target_pairs={{0,4},{4,8},{8,12},{1,5},{5,9},{9,13},{2,6},{6,10},{10,14},{3,7},{... | collective-permute-start | bytes 61448 | tf_op jit(solution)/shard_map/ppermute | solution.py:22
  18.1 44.8 %collective-permute-start.3 = (f32[20,2,128]{2,1,0:T(2,128)S(1)}, f32[20,2,128]{2,1,0:T(2,128)S(1)}, u32[]{:S(2)}, u32[]{:S(2)}) collective-permute-start(f32[20,2,128]{2,1,0:T(2,128)S(1)} %get-tuple-element.43), channel_id=1, source_target_pairs={{4,0},{8,4},{12,8},{5,1},{9,5},{13,9},{6,2},{10,6},{14,10},{7,3},{... | collective-permute-start | bytes 61448 | tf_op jit(solution)/shard_map/ppermute | solution.py:23
  63.8 9.0 %collective-permute-start.4 = (f32[20,20,2]{2,1,0:T(8,128)}, f32[20,20,2]{2,1,0:T(8,128)S(1)}, u32[]{:S(2)}, u32[]{:S(2)}) collective-permute-start(f32[20,20,2]{2,1,0:T(8,128)} %get-tuple-element.22), channel_id=1, source_target_pairs={{0,1},{1,2},{2,3},{4,5},{5,6},{6,7},{8,9},{9,10},{10,11},{12,13},{... | collective-permute-start | bytes 9608 | tf_op jit(solution)/shard_map/ppermute | solution.py:22
  67.1 8.7 %collective-permute-start.5 = (f32[20,20,2]{2,1,0:T(8,128)}, f32[20,20,2]{2,1,0:T(8,128)S(1)}, u32[]{:S(2)}, u32[]{:S(2)}) collective-permute-start(f32[20,20,2]{2,1,0:T(8,128)} %get-tuple-element.23), channel_id=1, source_target_pairs={{1,0},{2,1},{3,2},{5,4},{6,5},{7,6},{9,8},{10,9},{11,10},{13,12},{... | collective-permute-start | bytes 9608 | tf_op jit(solution)/shard_map/ppermute | solution.py:23
  93.9 8.0 %collective-permute-start.10 = (f32[18,18,1]{2,1,0:T(8,128)S(1)}, f32[18,18,1]{2,1,0:T(8,128)S(1)}, u32[]{:S(2)}, u32[]{:S(2)}) collective-permute-start(f32[18,18,1]{2,1,0:T(8,128)S(1)} %get-tuple-element.34), channel_id=1, source_target_pairs={{1,0},{2,1},{3,2},{5,4},{6,5},{7,6},{9,8},{10,9},{11,10},{13,12},{... | collective-permute-start | bytes 3896 | tf_op jit(solution)/shard_map/ppermute | solution.py:23
  106.3 44.7 %collective-permute-start.12 = (f32[2,16,128]{2,1,0:T(8,128)S(1)}, f32[2,16,128]{2,1,0:T(8,128)S(1)}, u32[]{:S(2)}, u32[]{:S(2)}) collective-permute-start(f32[2,16,128]{2,1,0:T(8,128)S(1)} %get-tuple-element.70), channel_id=1, source_target_pairs={{0,16},{1,17},{2,18},{3,19},{4,20},{5,21},{6,22},{7,23},{8,24},{9,... | collective-permute-start | bytes 49160 | tf_op jit(solution)/shard_map/ppermute | solution.py:22
  107.6 43.4 %collective-permute-start.13 = (f32[2,16,128]{2,1,0:T(8,128)S(1)}, f32[2,16,128]{2,1,0:T(8,128)S(1)}, u32[]{:S(2)}, u32[]{:S(2)}) collective-permute-start(f32[2,16,128]{2,1,0:T(8,128)S(1)} %get-tuple-element.71), channel_id=1, source_target_pairs={{16,0},{17,1},{18,2},{19,3},{20,4},{21,5},{22,6},{23,7},{24,8},{25... | collective-permute-start | bytes 49160 | tf_op jit(solution)/shard_map/ppermute | solution.py:23
  161.9 10.0 %collective-permute-start.16 = (f32[20,20,2]{2,1,0:T(8,128)}, f32[20,20,2]{2,1,0:T(8,128)S(1)}, u32[]{:S(2)}, u32[]{:S(2)}) collective-permute-start(f32[20,20,2]{2,1,0:T(8,128)} %get-tuple-element.20), channel_id=1, source_target_pairs={{0,1},{1,2},{2,3},{4,5},{5,6},{6,7},{8,9},{9,10},{10,11},{12,13},{... | collective-permute-start | bytes 9608 | tf_op jit(solution)/shard_map/ppermute | solution.py:22
  165.2 8.4 %collective-permute-start.17 = (f32[20,20,2]{2,1,0:T(8,128)}, f32[20,20,2]{2,1,0:T(8,128)}, u32[]{:S(2)}, u32[]{:S(2)}) collective-permute-start(f32[20,20,2]{2,1,0:T(8,128)} %get-tuple-element.21), channel_id=1, source_target_pairs={{1,0},{2,1},{3,2},{5,4},{6,5},{7,6},{9,8},{10,9},{11,10},{13,12},{... | collective-permute-start | bytes 9608 | tf_op jit(solution)/shard_map/ppermute | solution.py:23
  191.8 8.2 %collective-permute-start.22 = (f32[18,18,1]{2,1,0:T(8,128)S(1)}, f32[18,18,1]{2,1,0:T(8,128)S(1)}, u32[]{:S(2)}, u32[]{:S(2)}) collective-permute-start(f32[18,18,1]{2,1,0:T(8,128)S(1)} %get-tuple-element.32), channel_id=1, source_target_pairs={{1,0},{2,1},{3,2},{5,4},{6,5},{7,6},{9,8},{10,9},{11,10},{13,12},{... | collective-permute-start | bytes 3896 | tf_op jit(solution)/shard_map/ppermute | solution.py:23
  194.3 8.0 %collective-permute-start.23 = (f32[18,18,1]{2,1,0:T(8,128)S(1)}, f32[18,18,1]{2,1,0:T(8,128)S(1)}, u32[]{:S(2)}, u32[]{:S(2)}) collective-permute-start(f32[18,18,1]{2,1,0:T(8,128)S(1)} %get-tuple-element.33), channel_id=1, source_target_pairs={{0,1},{1,2},{2,3},{4,5},{5,6},{6,7},{8,9},{9,10},{10,11},{12,13},{... | collective-permute-start | bytes 3896 | tf_op jit(solution)/shard_map/ppermute | solution.py:22
  267.4 8.0 %collective-permute-start.28 = (f32[18,18,1]{2,1,0:T(8,128)S(1)}, f32[18,18,1]{2,1,0:T(8,128)S(1)}, u32[]{:S(2)}, u32[]{:S(2)}) collective-permute-start(f32[18,18,1]{2,1,0:T(8,128)S(1)} %get-tuple-element.30), channel_id=1, source_target_pairs={{1,0},{2,1},{3,2},{5,4},{6,5},{7,6},{9,8},{10,9},{11,10},{13,12},{... | collective-permute-start | bytes 3896 | tf_op jit(solution)/shard_map/ppermute | solution.py:23
  279.5 45.2 %collective-permute-start.30 = (f32[2,16,128]{2,1,0:T(8,128)S(1)}, f32[2,16,128]{2,1,0:T(8,128)S(1)}, u32[]{:S(2)}, u32[]{:S(2)}) collective-permute-start(f32[2,16,128]{2,1,0:T(8,128)S(1)} %get-tuple-element.64), channel_id=1, source_target_pairs={{0,16},{1,17},{2,18},{3,19},{4,20},{5,21},{6,22},{7,23},{8,24},{9,... | collective-permute-start | bytes 49160 | tf_op jit(solution)/shard_map/ppermute | solution.py:22
  280.8 43.9 %collective-permute-start.31 = (f32[2,16,128]{2,1,0:T(8,128)S(1)}, f32[2,16,128]{2,1,0:T(8,128)S(1)}, u32[]{:S(2)}, u32[]{:S(2)}) collective-permute-start(f32[2,16,128]{2,1,0:T(8,128)S(1)} %get-tuple-element.65), channel_id=1, source_target_pairs={{16,0},{17,1},{18,2},{19,3},{20,4},{21,5},{22,6},{23,7},{24,8},{25... | collective-permute-start | bytes 49160 | tf_op jit(solution)/shard_map/ppermute | solution.py:23
  335.5 9.6 %collective-permute-start.34 = (f32[20,20,2]{2,1,0:T(8,128)}, f32[20,20,2]{2,1,0:T(8,128)}, u32[]{:S(2)}, u32[]{:S(2)}) collective-permute-start(f32[20,20,2]{2,1,0:T(8,128)} %get-tuple-element.18), channel_id=1, source_target_pairs={{0,1},{1,2},{2,3},{4,5},{5,6},{6,7},{8,9},{9,10},{10,11},{12,13},{... | collective-permute-start | bytes 9608 | tf_op jit(solution)/shard_map/ppermute | solution.py:22
  338.8 8.4 %collective-permute-start.35 = (f32[20,20,2]{2,1,0:T(8,128)}, f32[20,20,2]{2,1,0:T(8,128)}, u32[]{:S(2)}, u32[]{:S(2)}) collective-permute-start(f32[20,20,2]{2,1,0:T(8,128)} %get-tuple-element.19), channel_id=1, source_target_pairs={{1,0},{2,1},{3,2},{5,4},{6,5},{7,6},{9,8},{10,9},{11,10},{13,12},{... | collective-permute-start | bytes 9608 | tf_op jit(solution)/shard_map/ppermute | solution.py:23
  364.9 8.2 %collective-permute-start.40 = (f32[18,18,1]{2,1,0:T(8,128)S(1)}, f32[18,18,1]{2,1,0:T(8,128)S(1)}, u32[]{:S(2)}, u32[]{:S(2)}) collective-permute-start(f32[18,18,1]{2,1,0:T(8,128)S(1)} %get-tuple-element.28), channel_id=1, source_target_pairs={{1,0},{2,1},{3,2},{5,4},{6,5},{7,6},{9,8},{10,9},{11,10},{13,12},{... | collective-permute-start | bytes 3896 | tf_op jit(solution)/shard_map/ppermute | solution.py:23
  378.1 44.3 %collective-permute-start.42 = (f32[2,16,128]{2,1,0:T(8,128)S(1)}, f32[2,16,128]{2,1,0:T(8,128)S(1)}, u32[]{:S(2)}, u32[]{:S(2)}) collective-permute-start(f32[2,16,128]{2,1,0:T(8,128)S(1)} %get-tuple-element.60), channel_id=1, source_target_pairs={{0,16},{1,17},{2,18},{3,19},{4,20},{5,21},{6,22},{7,23},{8,24},{9,... | collective-permute-start | bytes 49160 | tf_op jit(solution)/shard_map/ppermute | solution.py:22
  379.4 43.0 %collective-permute-start.43 = (f32[2,16,128]{2,1,0:T(8,128)S(1)}, f32[2,16,128]{2,1,0:T(8,128)S(1)}, u32[]{:S(2)}, u32[]{:S(2)}) collective-permute-start(f32[2,16,128]{2,1,0:T(8,128)S(1)} %get-tuple-element.61), channel_id=1, source_target_pairs={{16,0},{17,1},{18,2},{19,3},{20,4},{21,5},{22,6},{23,7},{24,8},{25... | collective-permute-start | bytes 49160 | tf_op jit(solution)/shard_map/ppermute | solution.py:23
  433.3 10.7 %collective-permute-start.46 = (f32[20,20,2]{2,1,0:T(8,128)}, f32[20,20,2]{2,1,0:T(8,128)}, u32[]{:S(2)}, u32[]{:S(2)}) collective-permute-start(f32[20,20,2]{2,1,0:T(8,128)} %get-tuple-element.16), channel_id=1, source_target_pairs={{0,1},{1,2},{2,3},{4,5},{5,6},{6,7},{8,9},{9,10},{10,11},{12,13},{... | collective-permute-start | bytes 9608 | tf_op jit(solution)/shard_map/ppermute | solution.py:22
  436.6 8.4 %collective-permute-start.47 = (f32[20,20,2]{2,1,0:T(8,128)}, f32[20,20,2]{2,1,0:T(8,128)}, u32[]{:S(2)}, u32[]{:S(2)}) collective-permute-start(f32[20,20,2]{2,1,0:T(8,128)} %get-tuple-element.17), channel_id=1, source_target_pairs={{1,0},{2,1},{3,2},{5,4},{6,5},{7,6},{9,8},{10,9},{11,10},{13,12},{... | collective-permute-start | bytes 9608 | tf_op jit(solution)/shard_map/ppermute | solution.py:23
  463.4 8.2 %collective-permute-start.52 = (f32[18,18,1]{2,1,0:T(8,128)S(1)}, f32[18,18,1]{2,1,0:T(8,128)S(1)}, u32[]{:S(2)}, u32[]{:S(2)}) collective-permute-start(f32[18,18,1]{2,1,0:T(8,128)S(1)} %get-tuple-element.26), channel_id=1, source_target_pairs={{1,0},{2,1},{3,2},{5,4},{6,5},{7,6},{9,8},{10,9},{11,10},{13,12},{... | collective-permute-start | bytes 3896 | tf_op jit(solution)/shard_map/ppermute | solution.py:23
  (42 other events, 272.0 us)
